TPU v7x, 256 devices: a whole 4x4x8 slice. The times are simulated.
256 devices in a mesh: region: 8 (over z), row: 32 (over y, x, core).
Axes of the slice: x: 4, y: 4, z: 8, core: 2. Of those that a mesh axis runs over, the one named last changes fastest.
Arguments:
- state0: float32 [32, 131072], P(None, ('region', 'row')), may hold values from -6 to 6
- drive: bfloat16 [32, 131072], P(None, ('region', 'row')), may hold values from -6 to 6
- cotangent: float32 [32, 131072], P(None, ('region', 'row')), may hold values from -6 to 6
- excitatory: int32 [131072], P(('region', 'row')), may hold values 0 or 1
- tile_vals: bfloat16 [1024, 24, 128, 128], P(('region', 'row')), may hold values from 0.0039978027 to 0.039794922
- tile_cols: int32 [1024, 24], P(('region', 'row')), may hold values from 0 to 159
- tile_count: int32 [1024], P(('region', 'row')), may hold values from 1 to 24, as said below
- boundary_rows: int32 [8, 32, 8, 16], P('region', 'row'), may hold values from 0 to 511, as said below
- u_factor: bfloat16 [32, 131072], P(None, ('region', 'row')), may hold values from -1 to 1
- v_factor: bfloat16 [32, 131072], P(None, ('region', 'row')), may hold values from -0.015625 to 0.015625
Outputs:
- final_state: float32 [32, 131072], P(None, ('region', 'row'))
- grad_u: float32 [32, 131072], P(None, ('region', 'row'))
- grad_v: float32 [32, 131072], P(None, ('region', 'row'))
Inputs may be any that keep to these rules, and one draw needn't show every extreme that they name: tile_count[q] tiles of row tile q are live; its tiles j >= tile_count[q] take no part; the most, 24, is reached in every draw. `boundary_rows`: the 16 rows of one list are distinct. tile_cols[q, j] numbers a tile of 128 extended columns of the group of row tile q.
All inputs are finite; a program needn't handle non-finite values. No bound on the sum of `excitatory` on one device may be relied on, other than what follows from the above.
Results may differ from a plain program's by a relative error of at most 0.0055.
Values may be sent and summed in bfloat16 or wider, within the bound.
No kernel may reach another device: no remote copies, remote signals or barrier semaphores. Data moves between devices by JAX's collectives and lax.ppermute only.
A program may use at most 64 MiB of HBM per device.

v0:
```python
import jax
import jax.numpy as jnp
from jax import lax
from jax.sharding import Mesh
from jax.sharding import PartitionSpec as P

STEPS = 4
ROW = ("row_0", "row_1", "row_2")
REGION_ROW = ("region", "row_0", "row_1", "row_2")
leak = 0.5


def apply_tiles(ext_cols, flat_cols, live_tiles, flat_tiles, row_tiles):
    batch_rows, span_cols = ext_cols.shape
    blocks = ext_cols.reshape(batch_rows, span_cols // 128, 128)[:, flat_cols, :]
    blocks = jnp.where(live_tiles[None, :, None], blocks, jnp.zeros((), blocks.dtype))
    product = jnp.einsum("bsk,sik->bsi", blocks, flat_tiles, preferred_element_type=jnp.float32)
    summed = product.reshape(batch_rows, row_tiles, -1, 128).sum(axis=2)
    return summed.reshape(batch_rows, row_tiles * 128)


def from_each_region(x, me):
    everyone = lax.all_gather(x, "region", axis=0, tiled=False)
    mine = lax.dynamic_index_in_dim(everyone, me, axis=2, keepdims=False)
    return jnp.moveaxis(mine, 0, 1).reshape(x.shape[0], -1)


def local(
    state0,
    drive,
    cotangent,
    excitatory,
    tile_vals,
    tile_cols,
    tile_count,
    boundary_rows,
    u_factor,
    v_factor,
):
    lanes = lax.axis_size(ROW)
    groups = lax.axis_size("region")
    me = lax.axis_index("region")
    own_rows = state0.shape[1]
    own_tiles = own_rows // 128
    row_tiles = tile_vals.shape[0]
    chosen = boundary_rows.reshape(-1)
    bound_cols = chosen.shape[0]
    bound_tiles = bound_cols // 128
    per_lane = own_tiles + bound_tiles
    lane_of = tile_cols // per_lane
    at_lane = tile_cols % per_lane
    remapped = jnp.where(
        at_lane < own_tiles,
        lane_of * own_tiles + at_lane,
        lanes * own_tiles + lane_of * bound_tiles + at_lane - own_tiles,
    )
    flat_cols = remapped.reshape(-1)
    live_grid = jnp.arange(tile_cols.shape[1], dtype=jnp.int32)[None, :] < tile_count[:, None]
    live_tiles = live_grid.reshape(-1)
    flat_tiles = tile_vals.reshape(-1, 128, 128)
    polarity = (2 * excitatory - 1).astype(jnp.float32)
    state = state0
    saved = []
    for moment in range(STEPS):
        rates = jnp.tanh(state)
        signed = (polarity * rates).astype(jnp.bfloat16)
        batch_rows = signed.shape[0]
        gathered_own = lax.all_gather(signed, ROW, axis=1, tiled=True)
        outgoing = jnp.take(signed, chosen, axis=1).reshape(batch_rows, groups, -1)
        incoming = from_each_region(outgoing, me)
        latent = lax.psum(
            jnp.dot(signed, v_factor.T, preferred_element_type=jnp.float32), REGION_ROW
        )
        gathered_border = lax.all_gather(incoming, ROW, axis=1, tiled=True)
        gathered = jnp.concatenate([gathered_own, gathered_border], axis=1)
        synaptic = apply_tiles(gathered, flat_cols, live_tiles, flat_tiles, row_tiles)
        latent_b = latent.astype(jnp.bfloat16)
        lowrank = jnp.dot(latent_b, u_factor, preferred_element_type=jnp.float32)
        saved.append((rates, signed, latent_b))
        state = state + leak * (-state + synaptic + lowrank + drive.astype(jnp.float32))
    grad_u = jnp.zeros((u_factor.shape[0], own_rows), jnp.float32)
    grad_v = jnp.zeros((v_factor.shape[0], own_rows), jnp.float32)
    adjoint = cotangent
    for moment in reversed(range(STEPS)):
        rates, signed, latent_b = saved[moment]
        scaled_b = (leak * adjoint).astype(jnp.bfloat16)
        coeffs = lax.psum(
            jnp.dot(scaled_b, u_factor.T, preferred_element_type=jnp.float32), REGION_ROW
        )
        coeffs_b = coeffs.astype(jnp.bfloat16)
        batch_rows = scaled_b.shape[0]
        spread = jnp.einsum(
            "bri,rjik->brjk",
            scaled_b.reshape(batch_rows, row_tiles, 128),
            tile_vals,
            preferred_element_type=jnp.float32,
        )
        spread = jnp.where(live_grid[None, :, :, None], spread, 0.0)
        columns = jnp.zeros((batch_rows, lanes * per_lane, 128), jnp.float32)
        columns = columns.at[:, flat_cols, :].add(spread.reshape(batch_rows, -1, 128))
        rounded = columns.astype(jnp.bfloat16).astype(jnp.float32)
        own_cols = rounded[:, : lanes * own_tiles].reshape(batch_rows, -1)
        border_cols = rounded[:, lanes * own_tiles :].reshape(batch_rows, -1)
        border = lax.psum_scatter(border_cols, ROW, scatter_dimension=1, tiled=True)
        returned = from_each_region(border.reshape(batch_rows, groups, -1), me)
        own_part = lax.psum_scatter(own_cols, ROW, scatter_dimension=1, tiled=True)
        through = own_part.at[:, chosen].add(returned)
        total_signed = through + jnp.dot(coeffs_b, v_factor, preferred_element_type=jnp.float32)
        grad_u = grad_u + jnp.dot(latent_b.T, scaled_b, preferred_element_type=jnp.float32)
        grad_v = grad_v + jnp.dot(coeffs_b.T, signed, preferred_element_type=jnp.float32)
        adjoint = (1.0 - leak) * adjoint + (1.0 - rates * rates) * polarity * total_signed
    return (state, grad_u, grad_v)


def solution(mesh):
    finer = Mesh(
        mesh.devices.reshape(mesh.shape["region"], 4, 4, 2), ("region", "row_0", "row_1", "row_2")
    )
    in_specs = (
        P(None, REGION_ROW),
        P(None, REGION_ROW),
        P(None, REGION_ROW),
        P(REGION_ROW),
        P(REGION_ROW, None, None, None),
        P(REGION_ROW, None),
        P(REGION_ROW),
        P("region", ROW, None, None),
        P(None, REGION_ROW),
        P(None, REGION_ROW),
    )
    out_specs = (P(None, REGION_ROW), P(None, REGION_ROW), P(None, REGION_ROW))
    return jax.shard_map(local, mesh=finer, in_specs=in_specs, out_specs=out_specs, check_vma=False)
```

profile of v0, /device:TPU:1, one launch (start us, length us, event | category | flops | bytes accessed | tf_op | source)
XLA Modules:
  0.0 1002.2 jit_solution(16985678666152582495)
XLA Ops:
  12.2 23.3 %all_gather.46 = bf16[8,32,8,16]{1,3,2,0:T(8,128)(2,1)S(1)} all-gather(bf16[1,32,8,16]{1,3,2,0:T(8,128)(2,1)S(1)} %bitcast.256), channel_id=1, replica_groups=mesh['region'=8,'row_0'=4,'row_1'=4,'row_2'=2] {'region'}, dimensions={0}, use_global_device_ids=true | all-gather | bytes 73728 | tf_op jit(solution)/shard_map/all_gather | solution.py:23
  38.0 81.1 %psum.56 = bf16[32,32]{1,0:T(8,128)(2,1)S(1)} all-reduce(f32[32,32]{1,0:T(8,128)S(1)} %fusion.61), channel_id=1, replica_groups=mesh['region'=8,'row_0'=4,'row_1'=4,'row_2'=2] {'region','row_0','row_1'..., use_global_device_ids=true, to_apply=%region_1.3 | all-reduce | flops 1024 | bytes 6144 | tf_op jit(solution)/shard_map/psum | solution.py:71
  119.2 24.4 %all_gather.47 = bf16[32,4096]{1,0:T(8,128)(2,1)S(1)} all-gather(bf16[32,128]{1,0:T(8,128)(2,1)S(1)} %copy.91), channel_id=1, replica_groups=mesh['region'=8,'row_0'=4,'row_1'=4,'row_2'=2] {'row_0','row_1','row_2'}, dimensions={1}, use_global_device_ids=true | all-gather | bytes 270336 | tf_op jit(solution)/shard_map/all_gather | solution.py:74
  149.0 4.1 fusion.18
  159.1 13.2 %scatter_fusion = f32[32,160,128]{2,0,1:T(8,128)} fusion(f32[32,160,128]{2,0,1:T(8,128)} %broadcast.101.clone, s32[96]{0:T(128)S(1)} %fusion.53, f32[96,32,128]{2,1,0:T(8,128)} %bitcast.243), kind=kCustom, calls=%fused_computation.8 | custom fusion | flops 393216 | bytes 4718976 | tf_op jit(solution)/shard_map/scatter-add | solution.py:100
  181.5 19.1 %all_gather.49 = bf16[8,32,8,16]{1,3,2,0:T(8,128)(2,1)S(1)} all-gather(bf16[1,32,8,16]{1,3,2,0:T(8,128)(2,1)S(1)} %bitcast.257), channel_id=1, replica_groups=mesh['region'=8,'row_0'=4,'row_1'=4,'row_2'=2] {'region'}, dimensions={0}, use_global_device_ids=true | all-gather | bytes 73728 | tf_op jit(solution)/shard_map/all_gather | solution.py:23
  201.4 77.0 %psum.57 = bf16[32,32]{1,0:T(8,128)(2,1)} all-reduce(f32[32,32]{1,0:T(8,128)S(1)} %fusion.62), channel_id=1, replica_groups=mesh['region'=8,'row_0'=4,'row_1'=4,'row_2'=2] {'region','row_0','row_1'..., use_global_device_ids=true, to_apply=%region_3.5 | all-reduce | flops 1024 | bytes 6144 | tf_op jit(solution)/shard_map/psum | solution.py:71
  278.4 24.3 %all_gather.50 = bf16[32,4096]{1,0:T(8,128)(2,1)S(1)} all-gather(bf16[32,128]{1,0:T(8,128)(2,1)} %copy.95), channel_id=1, replica_groups=mesh['region'=8,'row_0'=4,'row_1'=4,'row_2'=2] {'row_0','row_1','row_2'}, dimensions={1}, use_global_device_ids=true | all-gather | bytes 270336 | tf_op jit(solution)/shard_map/all_gather | solution.py:74
  308.4 4.2 fusion.16
  317.1 19.2 %all_gather.57 = f32[8,32,8,16]{1,3,2,0:T(8,128)S(1)} all-gather(f32[1,32,8,16]{1,3,2,0:T(8,128)S(1)} %bitcast.249), channel_id=1, replica_groups=mesh['region'=8,'row_0'=4,'row_1'=4,'row_2'=2] {'region'}, dimensions={0}, use_global_device_ids=true | all-gather | bytes 147456 | tf_op jit(solution)/shard_map/all_gather | solution.py:23
  338.7 19.3 %all_gather.52 = bf16[8,32,8,16]{1,3,2,0:T(8,128)(2,1)S(1)} all-gather(bf16[1,32,8,16]{1,3,2,0:T(8,128)(2,1)S(1)} %bitcast.258), channel_id=1, replica_groups=mesh['region'=8,'row_0'=4,'row_1'=4,'row_2'=2] {'region'}, dimensions={0}, use_global_device_ids=true | all-gather | bytes 73728 | tf_op jit(solution)/shard_map/all_gather | solution.py:23
  360.9 83.6 %all-reduce.1 = (bf16[32,32]{1,0:T(8,128)(2,1)}, bf16[32,32]{1,0:T(8,128)(2,1)S(1)}) all-reduce(f32[32,32]{1,0:T(8,128)S(1)} %fusion.63, f32[32,32]{1,0:T(8,128)} %fusion.65), channel_id=1, replica_groups=mesh['region'=8,'row_0'=4,'row_1'=4,'row_2'=2] {'region','row_0','row_1'..., use_global_device_ids=true, to_apply=%region_5.7 | all-reduce | flops 2048 | bytes 12288 | tf_op jit(solution)/shard_map/psum | solution.py:71
  450.3 24.4 %all_gather.53 = bf16[32,4096]{1,0:T(8,128)(2,1)S(1)} all-gather(bf16[32,128]{1,0:T(8,128)(2,1)} %copy.99), channel_id=1, replica_groups=mesh['region'=8,'row_0'=4,'row_1'=4,'row_2'=2] {'row_0','row_1','row_2'}, dimensions={1}, use_global_device_ids=true | all-gather | bytes 270336 | tf_op jit(solution)/shard_map/all_gather | solution.py:74
  491.6 13.2 %scatter_fusion.2 = f32[32,160,128]{2,0,1:T(8,128)} fusion(f32[32,160,128]{2,0,1:T(8,128)} %broadcast.101.clone.1, s32[96]{0:T(128)S(1)} %copy-done.35, f32[96,32,128]{2,1,0:T(8,128)} %bitcast.244), kind=kCustom, calls=%fused_computation.10 | custom fusion | flops 393216 | bytes 4718976 | tf_op jit(solution)/shard_map/scatter-add | solution.py:100
  512.4 73.7 %psum.61 = bf16[32,32]{1,0:T(8,128)(2,1)S(1)} all-reduce(f32[32,32]{1,0:T(8,128)S(1)} %fusion.66), channel_id=1, replica_groups=mesh['region'=8,'row_0'=4,'row_1'=4,'row_2'=2] {'region','row_0','row_1'..., use_global_device_ids=true, to_apply=%region_15.17 | all-reduce | flops 1024 | bytes 6144 | tf_op jit(solution)/shard_map/psum | solution.py:87
  588.7 21.2 %all_gather.58 = f32[8,32,8,16]{1,3,2,0:T(8,128)S(1)} all-gather(f32[1,32,8,16]{1,3,2,0:T(8,128)S(1)} %bitcast.250), channel_id=1, replica_groups=mesh['region'=8,'row_0'=4,'row_1'=4,'row_2'=2] {'region'}, dimensions={0}, use_global_device_ids=true | all-gather | bytes 147456 | tf_op jit(solution)/shard_map/all_gather | solution.py:23
  610.5 67.1 %reduce-scatter.11.cloned.1.call-done = f32[32,512]{1,0:T(8,128)} async-done(((f32[32,16384]{1,0:T(8,128)}), f32[32,512]{1,0:T(8,128)}) %reduce-scatter.11.cloned.1.call-update) | async-done | bytes 65552 | tf_op jit(solution)/shard_map/reduce_scatter | solution.py:106
  687.6 13.2 %scatter_fusion.4 = f32[32,160,128]{2,0,1:T(8,128)} fusion(f32[32,160,128]{2,0,1:T(8,128)} %broadcast.101, s32[96]{0:T(128)S(1)} %copy-done.36, f32[96,32,128]{2,1,0:T(8,128)} %bitcast.242), kind=kCustom, calls=%fused_computation.12 | custom fusion | flops 393216 | bytes 4718976 | tf_op jit(solution)/shard_map/scatter-add | solution.py:100
  710.0 20.6 %all_gather.55 = bf16[8,32,8,16]{1,3,2,0:T(8,128)(2,1)S(1)} all-gather(bf16[1,32,8,16]{1,3,2,0:T(8,128)(2,1)S(1)} %bitcast.255), channel_id=1, replica_groups=mesh['region'=8,'row_0'=4,'row_1'=4,'row_2'=2] {'region'}, dimensions={0}, use_global_device_ids=true | all-gather | bytes 73728 | tf_op jit(solution)/shard_map/all_gather | solution.py:23
  732.6 31.8 %all_gather.56 = bf16[32,4096]{1,0:T(8,128)(2,1)S(1)} all-gather(bf16[32,128]{1,0:T(8,128)(2,1)} %copy.103), channel_id=1, replica_groups=mesh['region'=8,'row_0'=4,'row_1'=4,'row_2'=2] {'row_0','row_1','row_2'}, dimensions={1}, use_global_device_ids=true | all-gather | bytes 270336 | tf_op jit(solution)/shard_map/all_gather | solution.py:74
  780.3 74.4 %psum.62 = bf16[32,32]{1,0:T(8,128)(2,1)S(1)} all-reduce(f32[32,32]{1,0:T(8,128)S(1)} %fusion.67), channel_id=1, replica_groups=mesh['region'=8,'row_0'=4,'row_1'=4,'row_2'=2] {'region','row_0','row_1'..., use_global_device_ids=true, to_apply=%region_20.22 | all-reduce | flops 1024 | bytes 6144 | tf_op jit(solution)/shard_map/psum | solution.py:87
  856.4 19.5 %all_gather.59 = f32[8,32,8,16]{1,3,2,0:T(8,128)S(1)} all-gather(f32[1,32,8,16]{1,3,2,0:T(8,128)S(1)} %bitcast.251), channel_id=1, replica_groups=mesh['region'=8,'row_0'=4,'row_1'=4,'row_2'=2] {'region'}, dimensions={0}, use_global_device_ids=true | all-gather | bytes 147456 | tf_op jit(solution)/shard_map/all_gather | solution.py:23
  876.5 28.5 %reduce-scatter.15.cloned.1.call-done = f32[32,512]{1,0:T(8,128)} async-done(((f32[32,16384]{1,0:T(8,128)}), f32[32,512]{1,0:T(8,128)}) %reduce-scatter.15.cloned.1.call-update) | async-done | bytes 65552 | tf_op jit(solution)/shard_map/reduce_scatter | solution.py:106
  911.1 77.4 %all-reduce = (bf16[32,32]{1,0:T(8,128)(2,1)S(1)}, bf16[32,32]{1,0:T(8,128)(2,1)S(1)}) all-reduce(f32[32,32]{1,0:T(8,128)} %fusion.64, f32[32,32]{1,0:T(8,128)S(1)} %fusion.68), channel_id=1, replica_groups=mesh['region'=8,'row_0'=4,'row_1'=4,'row_2'=2] {'region','row_0','row_1'..., use_global_device_ids=true, to_apply=%region_7.9 | all-reduce | flops 2048 | bytes 12288 | tf_op jit(solution)/shard_map/psum | solution.py:71
  (213 shorter events, 129.8 us)
Async XLA Ops:
  7.2 141.8 %copy-start = (bf16[4,24,128,128]{3,2,1,0:T(8,128)(2,1)S(1)}, bf16[4,24,128,128]{3,2,1,0:T(8,128)(2,1)}, u32[]{:S(2)}) copy-start(bf16[4,24,128,128]{3,2,1,0:T(8,128)(2,1)} %param.16) | copy-start | bytes 9437188
  7.2 136.4 %all-gather.5.cloned.1.call-start = ((), (), s32[]{:S(2)}) async-start(), calls=%async_computation.6 | async-start | bytes 1081344 | tf_op jit(solution)/shard_map/all_gather | solution.py:68
  9.6 293.2 %all-gather.7.cloned.1.call-start = ((), (), s32[]{:S(2)}) async-start(), calls=%async_computation.7 | async-start | bytes 1081344 | tf_op jit(solution)/shard_map/all_gather | solution.py:68
  12.1 169.3 %copy-start.31 = (pred[128]{0:T(512)(128)(4,1)}, pred[128]{0:T(512)(128)(4,1)S(1)}, u32[]{:S(2)}) copy-start(pred[128]{0:T(512)(128)(4,1)S(1)} %compare_and_fusion) | copy-start | bytes 388
  37.1 118.5 %copy-start.37 = (pred[4,24]{1,0:T(4,128)(4,1)}, pred[4,24]{1,0:T(4,128)(4,1)S(1)}, u32[]{:S(2)}) copy-start(pred[4,24]{1,0:T(4,128)(4,1)S(1)} %iota_compare_fusion) | copy-start | bytes 292
  37.1 111.8 %copy-start.28 = (pred[96]{0:T(512)(128)(4,1)}, pred[96]{0:T(512)(128)(4,1)S(1)}, u32[]{:S(2)}) copy-start(pred[96]{0:T(512)(128)(4,1)S(1)} %lt.81) | copy-start | bytes 292
  143.5 15.6 %copy-start.34 = (s32[96]{0:T(128)}, s32[96]{0:T(128)S(1)}, u32[]{:S(2)}) copy-start(s32[96]{0:T(128)S(1)} %fusion.53) | copy-start | bytes 1156
  155.5 160.8 %reduce-scatter.9.cloned.1.call-start = ((), (), s32[]{:S(2)}) async-start(), calls=%async_computation.11 | async-start | bytes 540672 | tf_op jit(solution)/shard_map/reduce_scatter | solution.py:104
  176.7 267.8 %reduce-scatter.7.cloned.1.call-start = ((), (), s32[]{:S(2)}) async-start(), calls=%async_computation.10 | async-start | bytes 2162688 | tf_op jit(solution)/shard_map/reduce_scatter | solution.py:106
  179.8 21.5 %copy-start.5 = (bf16[32,512]{1,0:T(8,128)(2,1)S(1)}, bf16[32,512]{1,0:T(8,128)(2,1)}, u32[]{:S(2)}) copy-start(bf16[32,512]{1,0:T(8,128)(2,1)} %param.21) | copy-start | bytes 98308
  179.8 294.9 %all-gather.9.cloned.1.call-start = ((), (), s32[]{:S(2)}) async-start(), calls=%async_computation.8 | async-start | bytes 1081344 | tf_op jit(solution)/shard_map/all_gather | solution.py:68
  308.4 6.6 copy-start.26
  308.4 7.2 copy-start.14
  312.5 26.0 %copy-start.32 = (pred[128]{0:T(512)(128)(4,1)S(1)}, pred[128]{0:T(512)(128)(4,1)}, u32[]{:S(2)}) copy-start(pred[128]{0:T(512)(128)(4,1)} %copy-done.31) | copy-start | bytes 388
  314.9 273.0 %reduce-scatter.13.cloned.1.call-start = ((), (), s32[]{:S(2)}) async-start(), calls=%async_computation.13 | async-start | bytes 540672 | tf_op jit(solution)/shard_map/reduce_scatter | solution.py:104
  487.4 24.9 %copy-start.15 = (bf16[32,512]{1,0:T(8,128)(2,1)}, bf16[32,512]{1,0:T(8,128)(2,1)S(1)}, u32[]{:S(2)}) copy-start(bf16[32,512]{1,0:T(8,128)(2,1)S(1)} %get-tuple-element.8) | copy-start | bytes 98308
  509.1 168.5 %reduce-scatter.11.cloned.1.call-start = ((), (), s32[]{:S(2)}) async-start(), calls=%async_computation.12 | async-start | bytes 2162688 | tf_op jit(solution)/shard_map/reduce_scatter | solution.py:106
  512.2 256.2 %all-gather.11.cloned.1.call-start = ((), (), s32[]{:S(2)}) async-start(), calls=%async_computation.9 | async-start | bytes 1081344 | tf_op jit(solution)/shard_map/all_gather | solution.py:68
  586.1 91.5 %copy-start.24 = (bf16[32,32]{1,0:T(8,128)(2,1)}, bf16[32,32]{1,0:T(8,128)(2,1)S(1)}, u32[]{:S(2)}) copy-start(bf16[32,32]{1,0:T(8,128)(2,1)S(1)} %psum.61) | copy-start | bytes 6148
  586.2 269.4 %reduce-scatter.17.cloned.1.call-start = ((), (), s32[]{:S(2)}) async-start(), calls=%async_computation.15 | async-start | bytes 540672 | tf_op jit(solution)/shard_map/reduce_scatter | solution.py:104
  705.2 199.8 %reduce-scatter.15.cloned.1.call-start = ((), (), s32[]{:S(2)}) async-start(), calls=%async_computation.14 | async-start | bytes 2162688 | tf_op jit(solution)/shard_map/reduce_scatter | solution.py:106
  773.9 80.8 %copy-start.7 = (bf16[32,512]{1,0:T(8,128)(2,1)S(1)}, bf16[32,512]{1,0:T(8,128)(2,1)}, u32[]{:S(2)}) copy-start(bf16[32,512]{1,0:T(8,128)(2,1)} %get-tuple-element.11) | copy-start | bytes 98308
  774.0 80.8 %copy-start.19 = (f32[32,512]{1,0:T(8,128)S(1)}, f32[32,512]{1,0:T(8,128)}, u32[]{:S(2)}) copy-start(f32[32,512]{1,0:T(8,128)} %convolution_add_fusion.2) | copy-start | bytes 196612
  778.1 129.5 %copy-start.38 = (s32[128]{0:T(128)S(1)}, s32[128]{0:T(128)}, u32[]{:S(2)}) copy-start(s32[128]{0:T(128)} %fusion.54) | copy-start | bytes 1540
  (25 other events, 96.5 us)
Sparse Core Ops, SparseCore 0:
  10.5 52.4 all-gather.4
  155.6 44.2 all-gather.6
  203.6 81.8 reduce-scatter.8
  289.2 85.9 reduce-scatter.6
  377.6 49.4 all-gather.8
  509.2 78.6 reduce-scatter.12
  591.7 85.8 reduce-scatter.10
  680.1 49.4 all-gather.10
  733.3 82.0 reduce-scatter.16
  819.1 85.8 reduce-scatter.14
where the time goes:
time: 1010 us; the launch traced here: 1000 us
  blocking collectives  714 us (71%)
  waiting for transfers between devices  97.5 us (10%)
  other arithmetic  74.2 us (7%)
  local copies, waits for them, and re-layouts  56 us (6%)
  matrix products  45.3 us (4%)
  between operations  14.6 us (1%)
    psum x4, blocking collectives, local(): lax.psum(jnp.dot(signed, v_factor.T, preferred_element_type=jnp.float32),...  319 us
    psum x2, blocking collectives, local(): lax.psum(jnp.dot(scaled_b, u_factor.T, preferred_element_type=jnp.float32...  148 us
    all_gather x7, blocking collectives, from_each_region(): everyone = lax.all_gather(x, 'region', axis=0, tiled=False)  142 us
    all_gather x4, blocking collectives, local(): gathered_border = lax.all_gather(incoming, ROW, axis=1, tiled=True)  105 us
    reduce_scatter x3, waiting for transfers between devices, local(): own_part = lax.psum_scatter(own_cols, ROW, scatter_dimension=1, tiled=True)  95.6 us
    scatter-add x3, other arithmetic, local(): columns.at[:, flat_cols, :].add(spread.reshape(batch_rows, -1, 128))  39.6 us
  transfers between devices with their start and end apart: 10, of which 3 were waited for; matrix products, arithmetic and copies ran while one was open for 11% of the time, Pallas kernels for 0%

commit v1 on v0

--- a/solution.py
+++ b/solution.py
@@ -84,9 +84,9 @@
     for moment in reversed(range(STEPS)):
         rates, signed, latent_b = saved[moment]
         scaled_b = (leak * adjoint).astype(jnp.bfloat16)
-        coeffs = lax.psum(
-            jnp.dot(scaled_b, u_factor.T, preferred_element_type=jnp.float32), REGION_ROW
-        )
+        part = jnp.dot(scaled_b, u_factor.T, preferred_element_type=jnp.float32)
+        shards = lax.all_gather(part, REGION_ROW)
+        coeffs = jnp.sum(shards, axis=0)
         coeffs_b = coeffs.astype(jnp.bfloat16)
         batch_rows = scaled_b.shape[0]
         spread = jnp.einsum(

time: 1010 us -> 1450 us (1.44)
  waiting for transfers between devices: 97.5 us -> 686 us
  blocking collectives: 714 us -> 564 us
    all_gather x0 -> x4, waiting for transfers between devices: none -> 317 us  [local(): shards = lax.all_gather(part, REGION_ROW)]
    reduce_scatter x3, waiting for transfers between devices: 95.6 us -> 248 us  [local(): own_part = lax.psum_scatter(own_cols, ROW, scatter_dimension=1, tiled=True)]
    psum x2 -> x0, blocking collectives: 148 us -> none  [local(): lax.psum(jnp.dot(scaled_b, u_factor.T, preferred_element_type=jnp.float32...]
    reduce_scatter x3, waiting for transfers between devices: 1.68 us -> 76.2 us  [local(): border = lax.psum_scatter(border_cols, ROW, scatter_dimension=1, tiled=True)]
    all_gather x4, waiting for transfers between devices: 0.03 us -> 43.2 us  [local(): gathered_own = lax.all_gather(signed, ROW, axis=1, tiled=True)]
  transfers between devices with their start and end apart: 10 -> 14, of which waited for: 3 -> 9; matrix products, arithmetic and copies ran while one was open for 11% -> 7% of each run, Pallas kernels for 0% -> 0%
where the time goes in v1:
time: 1450 us; the launch traced here: 1440 us
  waiting for transfers between devices  686 us (47%)
  blocking collectives  564 us (39%)
  other arithmetic  83.4 us (6%)
  local copies, waits for them, and re-layouts  52.8 us (4%)
  matrix products  42.8 us (3%)
  between operations  14.5 us (1%)
    psum x4, blocking collectives, local(): lax.psum(jnp.dot(signed, v_factor.T, preferred_element_type=jnp.float32),...  322 us
    all_gather x4, waiting for transfers between devices, local(): shards = lax.all_gather(part, REGION_ROW)  317 us
    reduce_scatter x3, waiting for transfers between devices, local(): own_part = lax.psum_scatter(own_cols, ROW, scatter_dimension=1, tiled=True)  248 us
    all_gather x7, blocking collectives, from_each_region(): everyone = lax.all_gather(x, 'region', axis=0, tiled=False)  145 us
    all_gather x4, blocking collectives, local(): gathered_border = lax.all_gather(incoming, ROW, axis=1, tiled=True)  97.1 us
    reduce_scatter x3, waiting for transfers between devices, local(): border = lax.psum_scatter(border_cols, ROW, scatter_dimension=1, tiled=True)  76.2 us
    all_gather x4, waiting for transfers between devices, local(): gathered_own = lax.all_gather(signed, ROW, axis=1, tiled=True)  43.2 us
    scatter-add x3, other arithmetic, local(): columns.at[:, flat_cols, :].add(spread.reshape(batch_rows, -1, 128))  39.7 us
  transfers between devices with their start and end apart: 14, of which 9 were waited for; matrix products, arithmetic and copies ran while one was open for 7% of the time, Pallas kernels for 0%

profile of v1, /device:TPU:1, one launch (start us, length us, event | category | flops | bytes accessed | tf_op | source)
XLA Modules:
  0.0 1444.4 jit_solution(14764983206433964775)
XLA Ops:
  12.2 23.3 %all_gather.70 = bf16[8,32,8,16]{1,3,2,0:T(8,128)(2,1)S(1)} all-gather(bf16[1,32,8,16]{1,3,2,0:T(8,128)(2,1)S(1)} %bitcast.264), channel_id=1, replica_groups=mesh['region'=8,'row_0'=4,'row_1'=4,'row_2'=2] {'region'}, dimensions={0}, use_global_device_ids=true | all-gather | bytes 73728 | tf_op jit(solution)/shard_map/all_gather | solution.py:23
  38.1 81.2 %psum.28 = bf16[32,32]{1,0:T(8,128)(2,1)S(1)} all-reduce(f32[32,32]{1,0:T(8,128)S(1)} %fusion.61), channel_id=1, replica_groups=mesh['region'=8,'row_0'=4,'row_1'=4,'row_2'=2] {'region','row_0','row_1'..., use_global_device_ids=true, to_apply=%region_1.3 | all-reduce | flops 1024 | bytes 6144 | tf_op jit(solution)/shard_map/psum | solution.py:71
  119.3 24.3 %all_gather.71 = bf16[32,4096]{1,0:T(8,128)(2,1)S(1)} all-gather(bf16[32,128]{1,0:T(8,128)(2,1)S(1)} %copy.91), channel_id=1, replica_groups=mesh['region'=8,'row_0'=4,'row_1'=4,'row_2'=2] {'row_0','row_1','row_2'}, dimensions={1}, use_global_device_ids=true | all-gather | bytes 270336 | tf_op jit(solution)/shard_map/all_gather | solution.py:74
  182.5 18.7 %all_gather.73 = bf16[8,32,8,16]{1,3,2,0:T(8,128)(2,1)S(1)} all-gather(bf16[1,32,8,16]{1,3,2,0:T(8,128)(2,1)S(1)} %bitcast.265), channel_id=1, replica_groups=mesh['region'=8,'row_0'=4,'row_1'=4,'row_2'=2] {'region'}, dimensions={0}, use_global_device_ids=true | all-gather | bytes 73728 | tf_op jit(solution)/shard_map/all_gather | solution.py:23
  202.0 77.4 %psum.29 = bf16[32,32]{1,0:T(8,128)(2,1)S(1)} all-reduce(f32[32,32]{1,0:T(8,128)S(1)} %fusion.62), channel_id=1, replica_groups=mesh['region'=8,'row_0'=4,'row_1'=4,'row_2'=2] {'region','row_0','row_1'..., use_global_device_ids=true, to_apply=%region_3.5 | all-reduce | flops 1024 | bytes 6144 | tf_op jit(solution)/shard_map/psum | solution.py:71
  279.4 24.4 %all_gather.74 = bf16[32,4096]{1,0:T(8,128)(2,1)S(1)} all-gather(bf16[32,128]{1,0:T(8,128)(2,1)} %copy.95), channel_id=1, replica_groups=mesh['region'=8,'row_0'=4,'row_1'=4,'row_2'=2] {'row_0','row_1','row_2'}, dimensions={1}, use_global_device_ids=true | all-gather | bytes 270336 | tf_op jit(solution)/shard_map/all_gather | solution.py:74
  316.8 20.3 %all_gather.83 = f32[8,32,8,16]{1,3,2,0:T(8,128)S(1)} all-gather(f32[1,32,8,16]{1,3,2,0:T(8,128)S(1)} %bitcast.257), channel_id=1, replica_groups=mesh['region'=8,'row_0'=4,'row_1'=4,'row_2'=2] {'region'}, dimensions={0}, use_global_device_ids=true | all-gather | bytes 147456 | tf_op jit(solution)/shard_map/all_gather | solution.py:23
  337.7 68.6 %all-gather.21.cloned.1.call-done = f32[8192,32]{1,0:T(8,128)} async-done(((f32[32,32]{1,0:T(8,128)}), f32[8192,32]{1,0:T(8,128)}) %all-gather.21.cloned.1.call-update) | async-done | bytes 1048592 | tf_op jit(solution)/shard_map/all_gather | solution.py:88
  408.9 82.8 %reduce-scatter.7.cloned.1.call-done = f32[32,512]{1,0:T(8,128)} async-done(((f32[32,16384]{1,0:T(8,128)}), f32[32,512]{1,0:T(8,128)}) %reduce-scatter.7.cloned.1.call-update) | async-done | bytes 65552 | tf_op jit(solution)/shard_map/reduce_scatter | solution.py:106
  498.5 20.5 %all_gather.76 = bf16[8,32,8,16]{1,3,2,0:T(8,128)(2,1)S(1)} all-gather(bf16[1,32,8,16]{1,3,2,0:T(8,128)(2,1)S(1)} %bitcast.266), channel_id=1, replica_groups=mesh['region'=8,'row_0'=4,'row_1'=4,'row_2'=2] {'region'}, dimensions={0}, use_global_device_ids=true | all-gather | bytes 73728 | tf_op jit(solution)/shard_map/all_gather | solution.py:23
  521.9 81.9 %psum.30 = bf16[32,32]{1,0:T(8,128)(2,1)S(1)} all-reduce(f32[32,32]{1,0:T(8,128)S(1)} %fusion.63), channel_id=1, replica_groups=mesh['region'=8,'row_0'=4,'row_1'=4,'row_2'=2] {'region','row_0','row_1'..., use_global_device_ids=true, to_apply=%region_5.7 | all-reduce | flops 1024 | bytes 6144 | tf_op jit(solution)/shard_map/psum | solution.py:71
  603.8 22.9 %all_gather.77 = bf16[32,4096]{1,0:T(8,128)(2,1)S(1)} all-gather(bf16[32,128]{1,0:T(8,128)(2,1)} %copy.99), channel_id=1, replica_groups=mesh['region'=8,'row_0'=4,'row_1'=4,'row_2'=2] {'row_0','row_1','row_2'}, dimensions={1}, use_global_device_ids=true | all-gather | bytes 270336 | tf_op jit(solution)/shard_map/all_gather | solution.py:74
  664.5 76.2 %reduce-scatter.13.cloned.1.call-done = f32[32,128]{1,0:T(8,128)} async-done(((f32[32,4096]{1,0:T(8,128)}), f32[32,128]{1,0:T(8,128)}) %reduce-scatter.13.cloned.1.call-update) | async-done | bytes 16400 | tf_op jit(solution)/shard_map/reduce_scatter | solution.py:104
  741.5 21.6 %all_gather.86 = f32[8,32,8,16]{1,3,2,0:T(8,128)S(1)} all-gather(f32[1,32,8,16]{1,3,2,0:T(8,128)S(1)} %bitcast.258), channel_id=1, replica_groups=mesh['region'=8,'row_0'=4,'row_1'=4,'row_2'=2] {'region'}, dimensions={0}, use_global_device_ids=true | all-gather | bytes 147456 | tf_op jit(solution)/shard_map/all_gather | solution.py:23
  763.7 97.4 %all-gather.23.cloned.1.call-done = f32[8192,32]{1,0:T(8,128)} async-done(((f32[32,32]{1,0:T(8,128)}), f32[8192,32]{1,0:T(8,128)}) %all-gather.23.cloned.1.call-update) | async-done | bytes 1048592 | tf_op jit(solution)/shard_map/all_gather | solution.py:88
  863.6 82.9 %reduce-scatter.11.cloned.1.call-done = f32[32,512]{1,0:T(8,128)} async-done(((f32[32,16384]{1,0:T(8,128)}), f32[32,512]{1,0:T(8,128)}) %reduce-scatter.11.cloned.1.call-update) | async-done | bytes 65552 | tf_op jit(solution)/shard_map/reduce_scatter | solution.py:106
  980.0 20.1 %all_gather.79 = bf16[8,32,8,16]{1,3,2,0:T(8,128)(2,1)S(1)} all-gather(bf16[1,32,8,16]{1,3,2,0:T(8,128)(2,1)S(1)} %bitcast.263), channel_id=1, replica_groups=mesh['region'=8,'row_0'=4,'row_1'=4,'row_2'=2] {'region'}, dimensions={0}, use_global_device_ids=true | all-gather | bytes 73728 | tf_op jit(solution)/shard_map/all_gather | solution.py:23
  1000.4 81.9 %psum.31 = bf16[32,32]{1,0:T(8,128)(2,1)} all-reduce(f32[32,32]{1,0:T(8,128)S(1)} %fusion.64), channel_id=1, replica_groups=mesh['region'=8,'row_0'=4,'row_1'=4,'row_2'=2] {'region','row_0','row_1'..., use_global_device_ids=true, to_apply=%region_7.9 | all-reduce | flops 1024 | bytes 6144 | tf_op jit(solution)/shard_map/psum | solution.py:71
  1082.3 25.4 %all_gather.80 = bf16[32,4096]{1,0:T(8,128)(2,1)} all-gather(bf16[32,128]{1,0:T(8,128)(2,1)S(1)} %copy.103), channel_id=1, replica_groups=mesh['region'=8,'row_0'=4,'row_1'=4,'row_2'=2] {'row_0','row_1','row_2'}, dimensions={1}, use_global_device_ids=true | all-gather | bytes 270336 | tf_op jit(solution)/shard_map/all_gather | solution.py:74
  1109.3 20.5 %all_gather.89 = f32[8,32,8,16]{1,3,2,0:T(8,128)S(1)} all-gather(f32[1,32,8,16]{1,3,2,0:T(8,128)S(1)} %bitcast.259), channel_id=1, replica_groups=mesh['region'=8,'row_0'=4,'row_1'=4,'row_2'=2] {'region'}, dimensions={0}, use_global_device_ids=true | all-gather | bytes 147456 | tf_op jit(solution)/shard_map/all_gather | solution.py:23
  1130.4 48.2 %all-gather.25.cloned.1.call-done = f32[8192,32]{1,0:T(8,128)} async-done(((f32[32,32]{1,0:T(8,128)}), f32[8192,32]{1,0:T(8,128)}) %all-gather.25.cloned.1.call-update) | async-done | bytes 1048592 | tf_op jit(solution)/shard_map/all_gather | solution.py:88
  1181.2 82.8 %reduce-scatter.15.cloned.1.call-done = f32[32,512]{1,0:T(8,128)} async-done(((f32[32,16384]{1,0:T(8,128)}), f32[32,512]{1,0:T(8,128)}) %reduce-scatter.15.cloned.1.call-update) | async-done | bytes 65552 | tf_op jit(solution)/shard_map/reduce_scatter | solution.py:106
  1272.8 43.1 %all-gather.19.cloned.1.call-done = bf16[32,16384]{1,0:T(8,128)(2,1)} async-done(((bf16[32,512]{1,0:T(8,128)(2,1)}), bf16[32,16384]{1,0:T(8,128)(2,1)}) %all-gather.19.cloned.1.call-update) | async-done | bytes 1048592 | tf_op jit(solution)/shard_map/all_gather | solution.py:68
  1331.6 103.0 %all-gather.27.cloned.1.call-done = f32[8192,32]{1,0:T(8,128)} async-done(((f32[32,32]{1,0:T(8,128)}), f32[8192,32]{1,0:T(8,128)}) %all-gather.27.cloned.1.call-update) | async-done | bytes 1048592 | tf_op jit(solution)/shard_map/all_gather | solution.py:88
  (243 shorter events, 180.5 us)
Async XLA Ops:
  7.2 141.9 %copy-start = (bf16[4,24,128,128]{3,2,1,0:T(8,128)(2,1)S(1)}, bf16[4,24,128,128]{3,2,1,0:T(8,128)(2,1)}, u32[]{:S(2)}) copy-start(bf16[4,24,128,128]{3,2,1,0:T(8,128)(2,1)} %param.16) | copy-start | bytes 9437188
  7.2 136.4 %all-gather.13.cloned.1.call-start = ((), (), s32[]{:S(2)}) async-start(), calls=%async_computation.6 | async-start | bytes 1081344 | tf_op jit(solution)/shard_map/all_gather | solution.py:68
  9.6 294.2 %all-gather.15.cloned.1.call-start = ((), (), s32[]{:S(2)}) async-start(), calls=%async_computation.7 | async-start | bytes 1081344 | tf_op jit(solution)/shard_map/all_gather | solution.py:68
  11.3 170.4 %copy-start.34 = (s32[1024]{0:T(1024)}, s32[1024]{0:T(1024)S(1)}, u32[]{:S(2)}) copy-start(s32[1024]{0:T(1024)S(1)} %pad_clamp_fusion.1) | copy-start | bytes 12292
  37.1 118.6 %copy-start.45 = (pred[4,24]{1,0:T(4,128)(4,1)}, pred[4,24]{1,0:T(4,128)(4,1)S(1)}, u32[]{:S(2)}) copy-start(pred[4,24]{1,0:T(4,128)(4,1)S(1)} %iota_compare_fusion) | copy-start | bytes 292
  37.2 111.9 %copy-start.35 = (pred[96]{0:T(512)(128)(4,1)}, pred[96]{0:T(512)(128)(4,1)S(1)}, u32[]{:S(2)}) copy-start(pred[96]{0:T(512)(128)(4,1)S(1)} %lt.81) | copy-start | bytes 292
  155.6 160.4 %reduce-scatter.9.cloned.1.call-start = ((), (), s32[]{:S(2)}) async-start(), calls=%async_computation.11 | async-start | bytes 540672 | tf_op jit(solution)/shard_map/reduce_scatter | solution.py:104
  176.8 229.5 %all-gather.21.cloned.1.call-start = ((), (), s32[]{:S(2)}) async-start(), calls=%async_computation.16 | async-start | bytes 4210688 | tf_op jit(solution)/shard_map/all_gather | solution.py:88
  177.7 314.0 %reduce-scatter.7.cloned.1.call-start = ((), (), s32[]{:S(2)}) async-start(), calls=%async_computation.10 | async-start | bytes 2162688 | tf_op jit(solution)/shard_map/reduce_scatter | solution.py:106
  180.9 445.9 %all-gather.17.cloned.1.call-start = ((), (), s32[]{:S(2)}) async-start(), calls=%async_computation.8 | async-start | bytes 1081344 | tf_op jit(solution)/shard_map/all_gather | solution.py:68
  315.8 424.8 %reduce-scatter.13.cloned.1.call-start = ((), (), s32[]{:S(2)}) async-start(), calls=%async_computation.13 | async-start | bytes 540672 | tf_op jit(solution)/shard_map/reduce_scatter | solution.py:104
  316.0 178.3 %copy-start.46 = (s32[128]{0:T(128)}, s32[128]{0:T(128)S(1)}, u32[]{:S(2)}) copy-start(s32[128]{0:T(128)S(1)} %fusion.54) | copy-start | bytes 1540
  406.3 92.0 %copy-start.40 = (pred[128]{0:T(512)(128)(4,1)S(1)}, pred[128]{0:T(512)(128)(4,1)}, u32[]{:S(2)}) copy-start(pred[128]{0:T(512)(128)(4,1)} %copy-done.38) | copy-start | bytes 388
  408.9 82.8 %copy-start.25 = (bf16[32,32]{1,0:T(8,128)(2,1)}, bf16[32,32]{1,0:T(8,128)(2,1)S(1)}, u32[]{:S(2)}) copy-start(bf16[32,32]{1,0:T(8,128)(2,1)S(1)} %reduce_sum.76) | copy-start | bytes 6148
  660.4 200.7 %all-gather.23.cloned.1.call-start = ((), (), s32[]{:S(2)}) async-start(), calls=%async_computation.17 | async-start | bytes 4210688 | tf_op jit(solution)/shard_map/all_gather | solution.py:88
  661.2 285.3 %reduce-scatter.11.cloned.1.call-start = ((), (), s32[]{:S(2)}) async-start(), calls=%async_computation.12 | async-start | bytes 2162688 | tf_op jit(solution)/shard_map/reduce_scatter | solution.py:106
  664.4 444.1 %reduce-scatter.17.cloned.1.call-start = ((), (), s32[]{:S(2)}) async-start(), calls=%async_computation.15 | async-start | bytes 540672 | tf_op jit(solution)/shard_map/reduce_scatter | solution.py:104
  863.6 82.9 %copy-start.27 = (bf16[32,32]{1,0:T(8,128)(2,1)}, bf16[32,32]{1,0:T(8,128)(2,1)S(1)}, u32[]{:S(2)}) copy-start(bf16[32,32]{1,0:T(8,128)(2,1)S(1)} %reduce_sum.77) | copy-start | bytes 6148
  974.2 204.5 %all-gather.25.cloned.1.call-start = ((), (), s32[]{:S(2)}) async-start(), calls=%async_computation.18 | async-start | bytes 4210688 | tf_op jit(solution)/shard_map/all_gather | solution.py:88
  975.0 289.0 %reduce-scatter.15.cloned.1.call-start = ((), (), s32[]{:S(2)}) async-start(), calls=%async_computation.14 | async-start | bytes 2162688 | tf_op jit(solution)/shard_map/reduce_scatter | solution.py:106
  978.1 129.6 %copy-start.26 = (bf16[32,32]{1,0:T(8,128)(2,1)S(1)}, bf16[32,32]{1,0:T(8,128)(2,1)}, u32[]{:S(2)}) copy-start(bf16[32,32]{1,0:T(8,128)(2,1)} %copy-done.25) | copy-start | bytes 6148
  978.2 337.7 %all-gather.19.cloned.1.call-start = ((), (), s32[]{:S(2)}) async-start(), calls=%async_computation.9 | async-start | bytes 1081344 | tf_op jit(solution)/shard_map/all_gather | solution.py:68
  978.9 455.6 %all-gather.27.cloned.1.call-start = ((), (), s32[]{:S(2)}) async-start(), calls=%async_computation.19 | async-start | bytes 4210688 | tf_op jit(solution)/shard_map/all_gather | solution.py:88
  1181.2 82.8 %copy-start.29 = (bf16[32,32]{1,0:T(8,128)(2,1)}, bf16[32,32]{1,0:T(8,128)(2,1)S(1)}, u32[]{:S(2)}) copy-start(bf16[32,32]{1,0:T(8,128)(2,1)S(1)} %reduce_sum.78) | copy-start | bytes 6148
  (37 other events, 366.7 us)
Sparse Core Ops, SparseCore 0:
  10.5 52.4 all-gather.12
  155.7 44.2 all-gather.14
  203.7 81.9 reduce-scatter.8
  289.7 116.5 all-gather.20
  410.0 81.6 reduce-scatter.6
  494.0 49.5 all-gather.16
  660.5 80.0 reduce-scatter.12
  744.2 116.7 all-gather.22
  864.9 81.5 reduce-scatter.10
  974.3 84.0 reduce-scatter.16
  1062.0 116.5 all-gather.24
  1182.3 81.5 reduce-scatter.14
  1266.4 49.4 all-gather.18
  1319.9 114.5 all-gather.26
